TPU v7x, 256 devices: a whole 4x4x8 slice. The times are simulated.
256 devices in a mesh: req: 32 (over x, z), mlp: 8 (over y, core).
Axes of the slice: x: 4, y: 4, z: 8, core: 2. Of those that a mesh axis runs over, the one named last changes fastest.
Arguments:
- x_pages: bfloat16 [1024, 8, 4096], P('req', None, 'mlp'), may hold values from -6 to 6
- page_owner: int32 [1024], P('req'), may hold values from 0 to 31, as said below
- request_id: int32 [8192], P('req'), may hold values from 0 to 8191, as said below
- adapter_table: int32 [8192], P('req'), may hold values from 0 to 63
- ln_gain: float32 [4096], replicated, may hold values from 0.5 to 1.5
- ln_bias: float32 [4096], replicated, may hold values from -3 to 3
- w_query: bfloat16 [4096, 2048], P('req', 'mlp'), may hold values from -0.09375 to 0.09375
- w_key: bfloat16 [4096, 2048], P('req', 'mlp'), may hold values from -0.09375 to 0.09375
- w_value: bfloat16 [4096, 2048], P('req', 'mlp'), may hold values from -0.09375 to 0.09375
- w_attn_out: bfloat16 [2048, 4096], P('mlp', 'req'), may hold values from -0.125 to 0.125
- down_query: bfloat16 [4096, 1024], P('mlp'), may hold values from -0.09375 to 0.09375
- up_query: bfloat16 [1024, 2048], P(None, 'mlp'), may hold values from -1.5 to 1.5
- down_value: bfloat16 [4096, 1024], P('mlp'), may hold values from -0.09375 to 0.09375
- up_value: bfloat16 [1024, 2048], P(None, 'mlp'), may hold values from -1.5 to 1.5
- w_fc_in: bfloat16 [4096, 8192], P('req', 'mlp'), may hold values from -0.09375 to 0.09375
- b_fc_in: float32 [8192], P('mlp'), may hold values from -3 to 3
- down_fc: bfloat16 [4096, 1024], P('mlp'), may hold values from -0.09375 to 0.09375
- up_fc: bfloat16 [1024, 8192], P(None, 'mlp'), may hold values from -1.5 to 1.5
- w_fc_out: bfloat16 [8192, 4096], P('mlp', 'req'), may hold values from -0.0625 to 0.0625
- b_fc_out: float32 [4096], P('mlp'), may hold values from -3 to 3
Outputs:
- out_pages: bfloat16 [1024, 8, 4096], P('req', None, 'mlp')
Inputs may be any that keep to these rules, and one draw needn't show every extreme that they name: `page_owner`: every owner receives exactly 32 pages, at most 2 of them from one device, and some device sends exactly 2 pages to some owner. `request_id`: ids never fall; every request lies inside one owner's block of 256 rows, and the ids of block k lie in k * 256 to k * 256 + 255; some request is 256 long.
All inputs are finite; a program needn't handle non-finite values.
Results may differ from a plain program's by a relative error of at most 0.006.
Values may be sent and summed in bfloat16 or wider, within the bound.
No kernel may reach another device: no remote copies, remote signals or barrier semaphores. Data moves between devices by JAX's collectives and lax.ppermute only.
A program may use at most 128 MiB of HBM per device.

v0:
```python
import jax
import jax.numpy as jnp
from jax import lax
from jax.sharding import PartitionSpec as P

HS = 256
ROT = 64
NAD = 64
R = 16
EPS = 1e-05


def gelu_tanh(v):
    return 0.5 * v * (1.0 + jnp.tanh(0.7978845608028654 * (v + 0.044715 * v * v * v)))


def rotate(block, pos):
    half = ROT // 2
    freq = jnp.power(10000.0, -jnp.arange(half).astype(jnp.float32) * 2.0 / ROT)
    angle = pos.astype(jnp.float32)[:, None, None] * freq[None, None, :]
    cosine = jnp.cos(angle)
    sine = jnp.sin(angle)
    even = block[:, :, 0:ROT:2]
    odd = block[:, :, 1:ROT:2]
    turned = jnp.stack([even * cosine - odd * sine, odd * cosine + even * sine], axis=-1)
    turned = turned.reshape(block.shape[0], block.shape[1], ROT)
    return jnp.concatenate([turned, block[:, :, ROT:]], axis=2)


def on_device(
    x_pages,
    page_owner,
    request_id,
    adapter_table,
    ln_gain,
    ln_bias,
    w_query,
    w_key,
    w_value,
    w_attn_out,
    down_query,
    up_query,
    down_value,
    up_value,
    w_fc_in,
    b_fc_in,
    down_fc,
    up_fc,
    w_fc_out,
    b_fc_out,
):
    groups = lax.axis_size("req")
    pg_dev = x_pages.shape[0]
    page_len = x_pages.shape[1]
    width_m = x_pages.shape[2]
    tok = request_id.shape[0]
    per_owner = pg_dev // groups + 1
    slots = groups * per_owner
    page_iota = jnp.arange(pg_dev)
    earlier = (page_owner[None, :] == page_owner[:, None]) & (
        page_iota[None, :] < page_iota[:, None]
    )
    rank = jnp.sum(earlier.astype(jnp.int32), axis=1)
    slot = page_owner * per_owner + rank
    place = (slot[None, :] == jnp.arange(slots)[:, None]).astype(jnp.bfloat16)
    flat_pages = x_pages.reshape(pg_dev, page_len * width_m)
    outgoing = jnp.dot(place, flat_pages, preferred_element_type=jnp.float32).astype(jnp.bfloat16)
    outgoing = outgoing.reshape(groups, per_owner, page_len * width_m)
    filled = jnp.sum(place, axis=1).reshape(groups, per_owner)
    arrived, marks = (
        lax.all_to_all(outgoing, "req", split_axis=0, concat_axis=0, tiled=True),
        lax.all_to_all(filled, "req", split_axis=0, concat_axis=0, tiled=True),
    )
    valid = marks.reshape(slots).astype(jnp.float32)
    position = jnp.cumsum(valid) - 1.0
    take = (
        (position[None, :] == jnp.arange(pg_dev).astype(jnp.float32)[:, None])
        & (valid[None, :] > 0.5)
    ).astype(jnp.bfloat16)
    own_x = jnp.dot(
        take, arrived.reshape(slots, page_len * width_m), preferred_element_type=jnp.float32
    )
    own_x = own_x.astype(jnp.bfloat16).reshape(tok, width_m)
    column = lax.axis_index("mlp") * width_m
    whole = lax.all_gather(own_x, "mlp", axis=1, tiled=True).astype(jnp.float32)
    mean = jnp.mean(whole, axis=1, keepdims=True)
    var = jnp.mean(jnp.square(whole - mean), axis=1, keepdims=True)
    full_ln = ((whole - mean) * lax.rsqrt(var + EPS) * ln_gain + ln_bias).astype(jnp.bfloat16)
    ln_m = lax.dynamic_slice_in_dim(full_ln, column, width_m, 1)
    local_req = request_id - lax.axis_index("req") * tok
    lookup = local_req[:, None] == jnp.arange(tok)[None, :]
    adapter = jnp.sum(jnp.where(lookup, adapter_table[None, :], 0), axis=1)
    onehot = (adapter[:, None] == jnp.arange(NAD)[None, :]).astype(jnp.float32)
    onehot_low = onehot.astype(jnp.bfloat16)

    def pick(down):
        spread = jnp.dot(ln_m, down, preferred_element_type=jnp.float32).reshape(tok, NAD, R)
        return jnp.sum(spread * onehot[:, :, None], axis=1)

    picked = lax.psum((pick(down_query), pick(down_value), pick(down_fc)), "mlp")

    def lift(chosen, up):
        expanded = (onehot_low[:, :, None] * chosen.astype(jnp.bfloat16)[:, None, :]).reshape(
            tok, NAD * R
        )
        return jnp.dot(expanded, up, preferred_element_type=jnp.float32)

    row_iota = jnp.arange(tok)
    start = jnp.sum((request_id[None, :] < request_id[:, None]).astype(jnp.int32), axis=1)
    pos = row_iota - start
    mask = (request_id[:, None] == request_id[None, :]) & (row_iota[None, :] <= row_iota[:, None])
    heads_w = w_query.shape[1]
    pieces = (
        lax.all_gather(w_query, "req", axis=0, tiled=True),
        lax.all_gather(w_key, "req", axis=0, tiled=True),
        lax.all_gather(w_value, "req", axis=0, tiled=True),
    )
    cols = full_ln
    base_q, base_k, base_v = tuple(
        [jnp.dot(cols, piece, preferred_element_type=jnp.float32) for piece in pieces]
    )
    query = rotate(
        (base_q + lift(picked[0], up_query)).reshape(tok, heads_w // HS, HS), pos
    ).astype(jnp.bfloat16)
    keys = rotate(base_k.reshape(tok, heads_w // HS, HS), pos).astype(jnp.bfloat16)
    value = (
        (base_v + lift(picked[1], up_value)).astype(jnp.bfloat16).reshape(tok, heads_w // HS, HS)
    )
    scores = jnp.einsum("qhd,khd->hqk", query, keys, preferred_element_type=jnp.float32) * HS ** (
        -0.5
    )
    scores = jnp.where(mask[None, :, :], scores, -1e30)
    top = jnp.max(scores, axis=2, keepdims=True)
    weights = jnp.exp(scores - top)
    probs = (weights / jnp.sum(weights, axis=2, keepdims=True)).astype(jnp.bfloat16)
    mixed_heads = jnp.einsum("hqk,khd->qhd", probs, value, preferred_element_type=jnp.float32)
    attn = mixed_heads.astype(jnp.bfloat16).reshape(tok, heads_w)
    cols = full_ln
    hidden_pre = jnp.dot(
        cols, lax.all_gather(w_fc_in, "req", axis=0, tiled=True), preferred_element_type=jnp.float32
    )
    hidden_pre = hidden_pre + lift(picked[2], up_fc) + b_fc_in
    hidden = gelu_tanh(hidden_pre).astype(jnp.bfloat16)
    pieces = (
        lax.all_gather(w_attn_out, "req", axis=1, tiled=True),
        lax.all_gather(w_fc_out, "req", axis=1, tiled=True),
    )
    part = jnp.dot(attn, pieces[0], preferred_element_type=jnp.float32) + jnp.dot(
        hidden, pieces[1], preferred_element_type=jnp.float32
    )
    shares = lax.psum_scatter(part, "mlp", scatter_dimension=1, tiled=True)
    result = (own_x.astype(jnp.float32) + shares + b_fc_out).astype(jnp.bfloat16)
    back_flat = result.reshape(pg_dev, page_len * width_m)
    leaving = jnp.dot(take.T, back_flat, preferred_element_type=jnp.float32).astype(jnp.bfloat16)
    leaving = leaving.reshape(groups, per_owner, page_len * width_m)
    returned = lax.all_to_all(leaving, "req", split_axis=0, concat_axis=0, tiled=True)
    pages_back = jnp.dot(
        place.T, returned.reshape(slots, page_len * width_m), preferred_element_type=jnp.float32
    )
    return pages_back.astype(jnp.bfloat16).reshape(pg_dev, page_len, width_m)


def solution(mesh):
    in_specs = (
        P("req", None, "mlp"),
        P("req"),
        P("req"),
        P("req"),
        P(),
        P(),
        P("req", "mlp"),
        P("req", "mlp"),
        P("req", "mlp"),
        P("mlp", "req"),
        P("mlp", None),
        P(None, "mlp"),
        P("mlp", None),
        P(None, "mlp"),
        P("req", "mlp"),
        P("mlp"),
        P("mlp", None),
        P(None, "mlp"),
        P("mlp", "req"),
        P("mlp"),
    )
    out_specs = P("req", None, "mlp")
    return jax.shard_map(
        on_device, mesh=mesh, in_specs=in_specs, out_specs=out_specs, check_vma=False
    )
```

profile of v0, /device:TPU:57, one launch (start us, length us, event | category | flops | bytes accessed | tf_op | source)
XLA Modules:
  0.0 669.1 jit_solution(17255531953203514862)
XLA Ops:
  6.5 1.0 convert_reduce_fusion.3
  7.5 0.7 multiply_add_fusion.1
  8.3 0.7 all_to_all.16
  9.0 10.6 %all-to-all-start = ((bf16[32,1,2]{2,1,0:T(2,128)(2,1)}), bf16[32,1,2]{2,1,0:T(2,128)(2,1)S(1)}, u32[]{:S(2)}, u32[]{:S(2)}) async-start(bf16[32,1,2]{2,1,0:T(2,128)(2,1)} %all_to_all.16), calls=%async_computation | async-start | bytes 32768 | tf_op jit(solution)/shard_map/all_to_all | solution.py:72
  19.7 1.0 copy.46
  21.1 1.1 reshape.339
  22.3 5.1 all-to-all-done
  27.4 4.7 all-to-all-start.1
  32.6 14.9 %all-to-all-done.1 = bf16[32,2,4096]{2,1,0:T(2,128)(2,1)S(1)} async-done(((bf16[32,2,4096]{2,1,0:T(2,128)(2,1)}), bf16[32,2,4096]{2,1,0:T(2,128)(2,1)S(1)}, u32[]{:S(2)}, u32[]{:S(2)}) %all-to-all-start.1) | async-done | bytes 524320 | tf_op jit(solution)/shard_map/all_to_all | solution.py:71
  48.1 0.8 reshape.341
  49.0 0.7 all-gather.12.cloned.1.call-update
  49.7 0.7 all-gather.14.cloned.1.call-update
  50.4 0.5 all-gather.10.cloned.1.call-update
  51.0 0.5 all-gather.18.cloned.1.call-update
  51.6 0.5 all-gather.20.cloned.1.call-update
  52.2 0.7 all-gather.16.cloned.1.call-update
  52.9 0.5 multiply_power_fusion
  53.8 21.0 %all-gather.8.cloned.1.call-done = bf16[256,4096]{1,0:T(8,128)(2,1)} async-done(((bf16[256,512]{1,0:T(8,128)(2,1)}), bf16[256,4096]{1,0:T(8,128)(2,1)}) %all-gather.8.cloned.1.call-update) | async-done | bytes 2097168 | tf_op jit(solution)/shard_map/all_gather | solution.py:85
  74.8 2.1 convert_reduce_fusion
  77.1 0.7 fusion.2
  77.8 1.0 fusion.5
  79.0 0.6 fusion.28
  79.6 1.4 copy-done.5
  81.0 0.6 fusion.24
  81.6 0.6 fusion.26
  82.2 0.4 multiply_reduce_fusion.1
  82.6 24.0 %all-reduce = (bf16[256,16]{0,1:T(8,128)(2,1)S(1)}, bf16[256,16]{0,1:T(8,128)(2,1)S(1)}, bf16[256,16]{0,1:T(8,128)(2,1)S(1)}) all-reduce(f32[256,16]{0,1:T(8,128)S(1)} %get-tuple-element.6, f32[256,16]{0,1:T(8,128)S(1)} %get-tuple-element.7, f32[256,16]{0,1:T(8,128)S(1)} %get-tuple-element.5), channel_id=1, replica_groups=mesh['req'=32,'mlp'=8] {'mlp'}, use_global_device_ids=true, to_apply=%region_14.15 | all-reduce | flops 12288 | bytes 73728 | tf_op jit(solution)/shard_map/psum | solution.py:100
  106.6 44.5 %all-gather.12.cloned.1.call-done = bf16[4096,256]{1,0:T(8,128)(2,1)} async-done(((bf16[128,256]{1,0:T(8,128)(2,1)}), bf16[4096,256]{1,0:T(8,128)(2,1)}) %all-gather.12.cloned.1.call-update) | async-done | bytes 2097168 | tf_op jit(solution)/shard_map/all_gather | solution.py:114
  151.1 3.2 fusion.85
  154.9 0.7 copy-done.7
  155.5 73.3 %all-gather.14.cloned.1.call-done = bf16[4096,256]{1,0:T(8,128)(2,1)} async-done(((bf16[128,256]{1,0:T(8,128)(2,1)}), bf16[4096,256]{1,0:T(8,128)(2,1)}) %all-gather.14.cloned.1.call-update) | async-done | bytes 2097168 | tf_op jit(solution)/shard_map/all_gather | solution.py:115
  228.8 3.1 convolution_bitcast_fusion
  232.0 0.8 fusion.61
  233.0 0.9 fusion.40
  234.3 72.1 %all-gather.10.cloned.1.call-done = bf16[4096,256]{1,0:T(8,128)(2,1)} async-done(((bf16[128,256]{1,0:T(8,128)(2,1)}), bf16[4096,256]{1,0:T(8,128)(2,1)}) %all-gather.10.cloned.1.call-update) | async-done | bytes 2097168 | tf_op jit(solution)/shard_map/all_gather | solution.py:116
  306.4 3.0 fusion.84
  309.8 97.4 %all-gather.18.cloned.1.call-done = bf16[4096,1024]{1,0:T(8,128)(2,1)} async-done(((bf16[128,1024]{1,0:T(8,128)(2,1)}), bf16[4096,1024]{1,0:T(8,128)(2,1)}) %all-gather.18.cloned.1.call-update) | async-done | bytes 8388624 | tf_op jit(solution)/shard_map/all_gather | solution.py:140
  407.2 7.3 %fusion.86 = f32[256,1024]{1,0:T(8,128)} fusion(bf16[256,4096]{1,0:T(8,128)(2,1)} %copy-done.1, bf16[4096,1024]{1,0:T(8,128)(2,1)} %all-gather.18.cloned.1.call-done), kind=kOutput, calls=%fused_computation.132 | convolution fusion | flops 2147483648 | bytes 11534336 | tf_op jit(solution)/shard_map/dot_general | solution.py:139
  414.5 92.1 %all-gather.20.cloned.1.call-done = bf16[1024,4096]{1,0:T(8,128)(2,1)} async-done(((bf16[1024,128]{1,0:T(8,128)(2,1)}), bf16[1024,4096]{1,0:T(8,128)(2,1)}) %all-gather.20.cloned.1.call-update) | async-done | bytes 8388624 | tf_op jit(solution)/shard_map/all_gather | solution.py:146
  506.6 8.9 %fusion.16 = f32[256,4096]{1,0:T(8,128)} fusion(bf16[1024,4096]{1,0:T(8,128)(2,1)} %all-gather.20.cloned.1.call-done, f32[256,1024]{1,0:T(8,128)} %fusion.86, bf16[256,1024]{0,1:T(8,128)(2,1)S(1)} %bitcast.65, bf16[1024,1024]{1,0:T(8,128)(2,1)S(1)} %copy-done, f32[1024]{0:T(1024)S(1)} %copy-done.12), kind=kOutput, calls=%fused_computation.33 | convolution fusion | flops 2687238144 | bytes 16257024 | tf_op jit(solution)/shard_map/dot_general | solution.py:148
  515.5 67.1 %all-gather.16.cloned.1.call-done = bf16[256,4096]{1,0:T(8,128)(2,1)} async-done(((bf16[256,128]{1,0:T(8,128)(2,1)}), bf16[256,4096]{1,0:T(8,128)(2,1)}) %all-gather.16.cloned.1.call-update) | async-done | bytes 2097168 | tf_op jit(solution)/shard_map/all_gather | solution.py:145
  582.6 5.7 convolution_add_fusion
  588.3 42.6 %reduce-scatter.2.cloned.1.call-done = f32[256,512]{1,0:T(8,128)} async-done(((f32[256,4096]{1,0:T(8,128)}), f32[256,512]{1,0:T(8,128)}) %reduce-scatter.2.cloned.1.call-update) | async-done | bytes 524304 | tf_op jit(solution)/shard_map/reduce_scatter | solution.py:151
  630.9 1.1 add_convert_fusion
  632.2 0.4 convolution_convert_fusion
  632.9 27.0 %all_to_all.20 = bf16[32,2,4096]{2,1,0:T(2,128)(2,1)} all-to-all(bf16[32,2,4096]{2,1,0:T(2,128)(2,1)S(1)} %reshape.349), channel_id=1, replica_groups=mesh['req'=32,'mlp'=8] {'req'}, dimensions={0} | all-to-all | bytes 1048576 | tf_op jit(solution)/shard_map/all_to_all | solution.py:156
  660.0 1.2 reshape.350
  661.5 0.8 copy.47
  (84 shorter events, 4.6 us)
Async XLA Ops:
  6.5 500.1 %copy-start = (bf16[1024,1024]{1,0:T(8,128)(2,1)S(1)}, bf16[1024,1024]{1,0:T(8,128)(2,1)}, u32[]{:S(2)}) copy-start(bf16[1024,1024]{1,0:T(8,128)(2,1)} %param.37) | copy-start | bytes 6291460
  8.2 23.9 %copy-start.15 = (s32[32]{0:T(128)}, s32[32]{0:T(128)S(1)}, u32[]{:S(2)}) copy-start(s32[32]{0:T(128)S(1)} %multiply_add_fusion.1) | copy-start | bytes 388
  9.0 18.3 %all-to-all-start = ((bf16[32,1,2]{2,1,0:T(2,128)(2,1)}), bf16[32,1,2]{2,1,0:T(2,128)(2,1)S(1)}, u32[]{:S(2)}, u32[]{:S(2)}) async-start(bf16[32,1,2]{2,1,0:T(2,128)(2,1)} %all_to_all.16), calls=%async_computation | async-start | bytes 32768 | tf_op jit(solution)/shard_map/all_to_all | solution.py:72
  22.3 31.2 %copy-start.13 = (s32[256]{0:T(256)S(1)}, s32[256]{0:T(256)}, u32[]{:S(2)}) copy-start(s32[256]{0:T(256)} %param.22) | copy-start | bytes 3076
  22.3 31.4 %copy-start.19 = (s32[256]{0:T(256)S(1)}, s32[256]{0:T(256)}, u32[]{:S(2)}) copy-start(s32[256]{0:T(256)} %param.23) | copy-start | bytes 3076
  27.4 20.2 %all-to-all-start.1 = ((bf16[32,2,4096]{2,1,0:T(2,128)(2,1)}), bf16[32,2,4096]{2,1,0:T(2,128)(2,1)S(1)}, u32[]{:S(2)}, u32[]{:S(2)}) async-start(bf16[32,2,4096]{2,1,0:T(2,128)(2,1)} %reshape.339), calls=%async_computation.1 | async-start | bytes 1048576 | tf_op jit(solution)/shard_map/all_to_all | solution.py:71
  32.0 42.8 %all-gather.8.cloned.1.call-start = ((), (), s32[]{:S(2)}) async-start(), calls=%async_computation.4 | async-start | bytes 2359296 | tf_op jit(solution)/shard_map/all_gather | solution.py:85
  32.1 21.5 %copy-start.17 = (f32[32]{0:T(128)}, f32[32]{0:T(128)S(1)}, u32[]{:S(2)}) copy-start(f32[32]{0:T(128)S(1)} %iota_convert_fusion) | copy-start | bytes 388
  48.9 102.2 %all-gather.12.cloned.1.call-start = ((), (), s32[]{:S(2)}) async-start(), calls=%async_computation.6 | async-start | bytes 2162688 | tf_op jit(solution)/shard_map/all_gather | solution.py:114
  49.7 179.2 %all-gather.14.cloned.1.call-start = ((), (), s32[]{:S(2)}) async-start(), calls=%async_computation.7 | async-start | bytes 2162688 | tf_op jit(solution)/shard_map/all_gather | solution.py:115
  50.4 256.0 %all-gather.10.cloned.1.call-start = ((), (), s32[]{:S(2)}) async-start(), calls=%async_computation.5 | async-start | bytes 2162688 | tf_op jit(solution)/shard_map/all_gather | solution.py:116
  51.0 356.2 %all-gather.18.cloned.1.call-start = ((), (), s32[]{:S(2)}) async-start(), calls=%async_computation.9 | async-start | bytes 8650752 | tf_op jit(solution)/shard_map/all_gather | solution.py:140
  51.6 455.1 %all-gather.20.cloned.1.call-start = ((), (), s32[]{:S(2)}) async-start(), calls=%async_computation.10 | async-start | bytes 8650752 | tf_op jit(solution)/shard_map/all_gather | solution.py:146
  52.1 530.4 %all-gather.16.cloned.1.call-start = ((), (), s32[]{:S(2)}) async-start(), calls=%async_computation.8 | async-start | bytes 2162688 | tf_op jit(solution)/shard_map/all_gather | solution.py:145
  52.9 578.0 %reduce-scatter.2.cloned.1.call-start = ((), (), s32[]{:S(2)}) async-start(), calls=%async_computation.11 | async-start | bytes 4718592 | tf_op jit(solution)/shard_map/reduce_scatter | solution.py:151
  74.8 2.2 copy-start.2
  74.8 2.9 copy-start.10
  74.8 2.9 copy-start.11
  77.8 1.2 copy-start.4
  79.0 2.6 copy-start.1
  79.0 2.0 copy-start.5
  79.0 2.6 copy-start.6
  151.1 3.3 copy-start.8
  154.8 0.7 copy-start.7
  306.4 3.0 copy-start.9
  309.8 196.8 %copy-start.12 = (f32[1024]{0:T(1024)S(1)}, f32[1024]{0:T(1024)}, u32[]{:S(2)}) copy-start(f32[1024]{0:T(1024)} %param.35) | copy-start | bytes 12292
  588.3 42.6 %copy-start.3 = (bf16[256,512]{1,0:T(8,128)(2,1)S(1)}, bf16[256,512]{1,0:T(8,128)(2,1)}, u32[]{:S(2)}) copy-start(bf16[256,512]{1,0:T(8,128)(2,1)} %reshape.341) | copy-start | bytes 786436
  588.3 42.6 %copy-start.14 = (f32[512]{0:T(512)S(1)}, f32[512]{0:T(512)}, u32[]{:S(2)}) copy-start(f32[512]{0:T(512)} %param.39) | copy-start | bytes 6148
  588.3 43.9 %copy-start.18 = (f32[32]{0:T(128)S(1)}, f32[32]{0:T(128)}, u32[]{:S(2)}) copy-start(f32[32]{0:T(128)} %copy-done.17) | copy-start | bytes 388
  632.2 29.1 %copy-start.16 = (s32[32]{0:T(128)S(1)}, s32[32]{0:T(128)}, u32[]{:S(2)}) copy-start(s32[32]{0:T(128)} %copy-done.15) | copy-start | bytes 388
Sparse Core Ops, SparseCore 0:
  49.0 25.7 all-gather.7
  77.4 73.6 all-gather.11
  153.7 75.0 all-gather.13
  231.3 75.0 all-gather.9
  308.9 98.2 all-gather.17
  409.5 97.0 all-gather.19
  509.1 73.4 all-gather.15
  588.4 42.4 reduce-scatter.1
where the time goes:
time: 670 us; the launch traced here: 669 us
  waiting for transfers between devices  534 us (80%)
  blocking collectives  51 us (8%)
  matrix products  35.3 us (5%)
  starting transfers between devices  15.6 us (2%)
  between operations  13.9 us (2%)
  local copies, waits for them, and re-layouts  10.2 us (2%)
  other arithmetic  9.33 us (1%)
    all_gather x1, waiting for transfers between devices, on_device(): lax.all_gather(w_fc_in, 'req', axis=0, tiled=True)  97.4 us
    all_gather x1, waiting for transfers between devices, on_device(): lax.all_gather(w_fc_out, 'req', axis=1, tiled=True)  92.1 us
    all_gather x1, waiting for transfers between devices, on_device(): lax.all_gather(w_key, 'req', axis=0, tiled=True)  73.3 us
    all_gather x1, waiting for transfers between devices, on_device(): lax.all_gather(w_value, 'req', axis=0, tiled=True)  72.1 us
    all_gather x1, waiting for transfers between devices, on_device(): lax.all_gather(w_attn_out, 'req', axis=1, tiled=True)  67.1 us
    all_gather x1, waiting for transfers between devices, on_device(): lax.all_gather(w_query, 'req', axis=0, tiled=True)  44.5 us
    reduce_scatter x1, waiting for transfers between devices, on_device(): shares = lax.psum_scatter(part, 'mlp', scatter_dimension=1, tiled=True)  42.6 us
    all_to_all x1, blocking collectives, on_device(): lax.all_to_all(leaving, 'req', split_axis=0, concat_axis=0, tiled=True)  27 us
  transfers between devices with their start and end apart: 10, of which 10 were waited for; matrix products, arithmetic and copies ran while one was open for 6% of the time, Pallas kernels for 0%

commit v1 on v0

--- a/solution.py
+++ b/solution.py
@@ -8,6 +8,27 @@
 NAD = 64
 R = 16
 EPS = 1e-05
+
+
+def collect(x, axis, dim):
+    size, position, rows = (lax.axis_size(axis), lax.axis_index(axis), x.shape[dim])
+    right = [(i, (i + 1) % size) for i in range(size)]
+    backward = [(i, (i - 1) % size) for i in range(size)]
+    result = jnp.zeros((*x.shape[:dim], size * rows, *x.shape[dim + 1 :]), x.dtype)
+    result = lax.dynamic_update_slice_in_dim(result, x, position * rows, axis=dim)
+    from_left = from_right = x
+    half = size // 2
+    for step in range(1, half + 1):
+        from_left = lax.ppermute(from_left, axis, right)
+        result = lax.dynamic_update_slice_in_dim(
+            result, from_left, (position - step) % size * rows, axis=dim
+        )
+        if step < size - half:
+            from_right = lax.ppermute(from_right, axis, backward)
+            result = lax.dynamic_update_slice_in_dim(
+                result, from_right, (position + step) % size * rows, axis=dim
+            )
+    return result
 
 
 def gelu_tanh(v):
@@ -82,7 +103,7 @@
     )
     own_x = own_x.astype(jnp.bfloat16).reshape(tok, width_m)
     column = lax.axis_index("mlp") * width_m
-    whole = lax.all_gather(own_x, "mlp", axis=1, tiled=True).astype(jnp.float32)
+    whole = collect(own_x, "mlp", 1).astype(jnp.float32)
     mean = jnp.mean(whole, axis=1, keepdims=True)
     var = jnp.mean(jnp.square(whole - mean), axis=1, keepdims=True)
     full_ln = ((whole - mean) * lax.rsqrt(var + EPS) * ln_gain + ln_bias).astype(jnp.bfloat16)

time: 670 us -> 604 us (0.901)
  waiting for transfers between devices: 534 us -> 450 us
  starting transfers between devices: 15.6 us -> 29.6 us
    all_gather x1, waiting for transfers between devices: 44.5 us -> 0.02 us  [on_device(): lax.all_gather(w_query, 'req', axis=0, tiled=True)]
    all_gather x1, waiting for transfers between devices: 73.3 us -> 42.9 us  [on_device(): lax.all_gather(w_key, 'req', axis=0, tiled=True)]
    all_gather x1 -> x0, waiting for transfers between devices: 21 us -> none  [on_device(): whole = lax.all_gather(own_x, 'mlp', axis=1, tiled=True).astype(jnp.float32)]
    ppermute x0 -> x7, starting transfers between devices: none -> 14.1 us  [the longest x4 14 us: collect(): from_left = lax.ppermute(from_left, axis, right)]
    ppermute x0 -> x7, waiting for transfers between devices: none -> 11.9 us  [the longest x4 9.76 us: collect(): from_left = lax.ppermute(from_left, axis, right)]
    all_gather x1, waiting for transfers between devices: 92.1 us -> 99.4 us  [on_device(): lax.all_gather(w_fc_out, 'req', axis=1, tiled=True)]
  transfers between devices with their start and end apart: 10 -> 16, of which waited for: 10 -> 14; matrix products, arithmetic and copies ran while one was open for 6% -> 7% of each run, Pallas kernels for 0% -> 0%
where the time goes in v1:
time: 604 us; the launch traced here: 603 us
  waiting for transfers between devices  450 us (75%)
  blocking collectives  52.3 us (9%)
  matrix products  35.7 us (6%)
  starting transfers between devices  29.6 us (5%)
  local copies, waits for them, and re-layouts  14.1 us (2%)
  between operations  14 us (2%)
  other arithmetic  7.54 us (1%)
    all_gather x1, waiting for transfers between devices, on_device(): lax.all_gather(w_fc_out, 'req', axis=1, tiled=True)  99.4 us
    all_gather x1, waiting for transfers between devices, on_device(): lax.all_gather(w_fc_in, 'req', axis=0, tiled=True)  97.5 us
    all_gather x1, waiting for transfers between devices, on_device(): lax.all_gather(w_value, 'req', axis=0, tiled=True)  68.2 us
    all_gather x1, waiting for transfers between devices, on_device(): lax.all_gather(w_attn_out, 'req', axis=1, tiled=True)  62.7 us
    all_gather x1, waiting for transfers between devices, on_device(): lax.all_gather(w_key, 'req', axis=0, tiled=True)  42.9 us
    reduce_scatter x1, waiting for transfers between devices, on_device(): shares = lax.psum_scatter(part, 'mlp', scatter_dimension=1, tiled=True)  42.6 us
    all_to_all x1, blocking collectives, on_device(): lax.all_to_all(leaving, 'req', split_axis=0, concat_axis=0, tiled=True)  27 us
    psum x1, blocking collectives, on_device(): lax.psum((pick(down_query), pick(down_value), pick(down_fc)), 'mlp')  25.2 us
  transfers between devices with their start and end apart: 16, of which 14 were waited for; matrix products, arithmetic and copies ran while one was open for 7% of the time, Pallas kernels for 0%

profile of v1, /device:TPU:57, one launch (start us, length us, event | category | flops | bytes accessed | tf_op | source)
XLA Modules:
  0.0 603.0 jit_solution(16023295845801448230)
XLA Ops:
  6.5 0.7 all-gather.9.cloned.1.call-update
  9.9 0.9 convert_reduce_fusion.3
  11.6 0.7 all_to_all.16
  12.3 10.6 %all-to-all-start = ((bf16[32,1,2]{2,1,0:T(2,128)(2,1)}), bf16[32,1,2]{2,1,0:T(2,128)(2,1)S(1)}, u32[]{:S(2)}, u32[]{:S(2)}) async-start(bf16[32,1,2]{2,1,0:T(2,128)(2,1)} %all_to_all.16), calls=%async_computation | async-start | bytes 32768 | tf_op jit(solution)/shard_map/all_to_all | solution.py:93
  23.0 1.0 copy.46
  24.4 1.1 reshape.339
  25.6 5.1 all-to-all-done
  30.7 4.7 all-to-all-start.1
  36.7 15.6 %all-to-all-done.1 = bf16[32,2,4096]{2,1,0:T(2,128)(2,1)S(1)} async-done(((bf16[32,2,4096]{2,1,0:T(2,128)(2,1)}), bf16[32,2,4096]{2,1,0:T(2,128)(2,1)S(1)}, u32[]{:S(2)}, u32[]{:S(2)}) %all-to-all-start.1) | async-done | bytes 524320 | tf_op jit(solution)/shard_map/all_to_all | solution.py:92
  53.0 2.9 collective-permute-start
  56.1 3.0 collective-permute-done
  59.2 3.7 collective-permute-start.2
  63.7 2.5 collective-permute-done.2
  66.2 3.7 collective-permute-start.4
  69.9 0.9 collective-permute-done.3
  70.9 2.3 collective-permute-done.4
  73.2 3.7 collective-permute-start.6
  76.9 1.3 collective-permute-done.5
  78.3 1.9 collective-permute-done.6
  81.4 1.0 fusion.5
  83.1 1.4 copy-done.3
  86.2 25.2 %all-reduce = (bf16[256,16]{0,1:T(8,128)(2,1)S(1)}, bf16[256,16]{0,1:T(8,128)(2,1)S(1)}, bf16[256,16]{0,1:T(8,128)(2,1)S(1)}) all-reduce(f32[256,16]{0,1:T(8,128)S(1)} %get-tuple-element.6, f32[256,16]{0,1:T(8,128)S(1)} %get-tuple-element.7, f32[256,16]{0,1:T(8,128)S(1)} %get-tuple-element.5), channel_id=1, replica_groups=mesh['req'=32,'mlp'=8] {'mlp'}, use_global_device_ids=true, to_apply=%region_14.15 | all-reduce | flops 12288 | bytes 73728 | tf_op jit(solution)/shard_map/psum | solution.py:121
  111.5 1.0 fusion.83
  112.6 1.0 fusion.82
  113.6 0.7 fusion.84
  114.4 3.9 fusion.8
  118.2 0.9 slice.20
  119.1 0.9 slice.21
  119.9 42.9 %all-gather.11.cloned.1.call-done = bf16[4096,256]{1,0:T(8,128)(2,1)} async-done(((bf16[128,256]{1,0:T(8,128)(2,1)}), bf16[4096,256]{1,0:T(8,128)(2,1)}) %all-gather.11.cloned.1.call-update) | async-done | bytes 2097168 | tf_op jit(solution)/shard_map/all_gather | solution.py:136
  162.9 3.9 convolution_bitcast_fusion
  166.7 0.8 slice.23
  167.6 0.9 slice.24
  168.5 0.8 fusion.59
  169.4 0.9 fusion.38
  170.4 0.9 fusion.39
  171.6 0.7 copy-done.7
  172.4 68.2 %all-gather.7.cloned.1.call-done = bf16[4096,256]{1,0:T(8,128)(2,1)} async-done(((bf16[128,256]{1,0:T(8,128)(2,1)}), bf16[4096,256]{1,0:T(8,128)(2,1)}) %all-gather.7.cloned.1.call-update) | async-done | bytes 2097168 | tf_op jit(solution)/shard_map/all_gather | solution.py:137
  240.6 3.3 fusion.10
  243.9 97.5 %all-gather.15.cloned.1.call-done = bf16[4096,1024]{1,0:T(8,128)(2,1)} async-done(((bf16[128,1024]{1,0:T(8,128)(2,1)}), bf16[4096,1024]{1,0:T(8,128)(2,1)}) %all-gather.15.cloned.1.call-update) | async-done | bytes 8388624 | tf_op jit(solution)/shard_map/all_gather | solution.py:161
  341.4 99.4 %all-gather.17.cloned.1.call-done = bf16[1024,4096]{1,0:T(8,128)(2,1)} async-done(((bf16[1024,128]{1,0:T(8,128)(2,1)}), bf16[1024,4096]{1,0:T(8,128)(2,1)}) %all-gather.17.cloned.1.call-update) | async-done | bytes 8388624 | tf_op jit(solution)/shard_map/all_gather | solution.py:167
  440.8 13.1 %fusion.16 = f32[256,4096]{1,0:T(8,128)} fusion(bf16[1024,4096]{1,0:T(8,128)(2,1)} %all-gather.17.cloned.1.call-done, f32[256,1024]{1,0:T(8,128)S(1)} %fusion.84, bf16[256,4096]{1,0:T(8,128)(2,1)} %copy-done.1, bf16[4096,1024]{1,0:T(8,128)(2,1)} %all-gather.15.cloned.1.call-done, f32[1024]{0:T(1024)} %param.35), kind=kOutput, calls=%fused_computation.33 | convolution fusion | flops 4297850880 | bytes 24121344 | tf_op jit(solution)/shard_map/dot_general | solution.py:169
  453.9 62.7 %all-gather.13.cloned.1.call-done = bf16[256,4096]{1,0:T(8,128)(2,1)} async-done(((bf16[256,128]{1,0:T(8,128)(2,1)}), bf16[256,4096]{1,0:T(8,128)(2,1)}) %all-gather.13.cloned.1.call-update) | async-done | bytes 2097168 | tf_op jit(solution)/shard_map/all_gather | solution.py:166
  516.6 5.5 convolution_add_fusion
  522.1 42.6 %reduce-scatter.2.cloned.1.call-done = f32[256,512]{1,0:T(8,128)} async-done(((f32[256,4096]{1,0:T(8,128)}), f32[256,512]{1,0:T(8,128)}) %reduce-scatter.2.cloned.1.call-update) | async-done | bytes 524304 | tf_op jit(solution)/shard_map/reduce_scatter | solution.py:172
  564.7 1.1 add_convert_fusion
  566.8 27.0 %all_to_all.20 = bf16[32,2,4096]{2,1,0:T(2,128)(2,1)} all-to-all(bf16[32,2,4096]{2,1,0:T(2,128)(2,1)S(1)} %reshape.349), channel_id=1, replica_groups=mesh['req'=32,'mlp'=8] {'req'}, dimensions={0} | all-to-all | bytes 1048576 | tf_op jit(solution)/shard_map/all_to_all | solution.py:177
  593.8 1.2 reshape.350
  595.3 0.8 copy.47
  (98 shorter events, 12.1 us)
Async XLA Ops:
  6.5 107.1 %copy-start = (bf16[1024,1024]{1,0:T(8,128)(2,1)S(1)}, bf16[1024,1024]{1,0:T(8,128)(2,1)}, u32[]{:S(2)}) copy-start(bf16[1024,1024]{1,0:T(8,128)(2,1)} %param.37) | copy-start | bytes 6291460
  6.5 107.8 %all-gather.9.cloned.1.call-start = ((), (), s32[]{:S(2)}) async-start(), calls=%async_computation.5 | async-start | bytes 2162688 | tf_op jit(solution)/shard_map/all_gather | solution.py:135
  7.3 28.7 %copy-start.10 = (s32[256]{0:T(256)S(1)}, s32[256]{0:T(256)}, u32[]{:S(2)}) copy-start(s32[256]{0:T(256)} %param.22) | copy-start | bytes 3076
  7.3 28.8 %copy-start.16 = (s32[256]{0:T(256)S(1)}, s32[256]{0:T(256)}, u32[]{:S(2)}) copy-start(s32[256]{0:T(256)} %param.23) | copy-start | bytes 3076
  7.3 155.6 %all-gather.11.cloned.1.call-start = ((), (), s32[]{:S(2)}) async-start(), calls=%async_computation.6 | async-start | bytes 2162688 | tf_op jit(solution)/shard_map/all_gather | solution.py:136
  8.0 232.6 %all-gather.7.cloned.1.call-start = ((), (), s32[]{:S(2)}) async-start(), calls=%async_computation.4 | async-start | bytes 2162688 | tf_op jit(solution)/shard_map/all_gather | solution.py:137
  8.8 332.6 %all-gather.15.cloned.1.call-start = ((), (), s32[]{:S(2)}) async-start(), calls=%async_computation.8 | async-start | bytes 8650752 | tf_op jit(solution)/shard_map/all_gather | solution.py:161
  9.3 431.5 %all-gather.17.cloned.1.call-start = ((), (), s32[]{:S(2)}) async-start(), calls=%async_computation.9 | async-start | bytes 8650752 | tf_op jit(solution)/shard_map/all_gather | solution.py:167
  11.5 25.2 %copy-start.12 = (s32[32]{0:T(128)}, s32[32]{0:T(128)S(1)}, u32[]{:S(2)}) copy-start(s32[32]{0:T(128)S(1)} %multiply_add_fusion.1) | copy-start | bytes 388
  12.3 18.4 %all-to-all-start = ((bf16[32,1,2]{2,1,0:T(2,128)(2,1)}), bf16[32,1,2]{2,1,0:T(2,128)(2,1)S(1)}, u32[]{:S(2)}, u32[]{:S(2)}) async-start(bf16[32,1,2]{2,1,0:T(2,128)(2,1)} %all_to_all.16), calls=%async_computation | async-start | bytes 32768 | tf_op jit(solution)/shard_map/all_to_all | solution.py:93
  30.7 21.7 %all-to-all-start.1 = ((bf16[32,2,4096]{2,1,0:T(2,128)(2,1)}), bf16[32,2,4096]{2,1,0:T(2,128)(2,1)S(1)}, u32[]{:S(2)}, u32[]{:S(2)}) async-start(bf16[32,2,4096]{2,1,0:T(2,128)(2,1)} %reshape.339), calls=%async_computation.1 | async-start | bytes 1048576 | tf_op jit(solution)/shard_map/all_to_all | solution.py:92
  35.3 481.3 %all-gather.13.cloned.1.call-start = ((), (), s32[]{:S(2)}) async-start(), calls=%async_computation.7 | async-start | bytes 2162688 | tf_op jit(solution)/shard_map/all_gather | solution.py:166
  35.9 528.8 %reduce-scatter.2.cloned.1.call-start = ((), (), s32[]{:S(2)}) async-start(), calls=%async_computation.10 | async-start | bytes 4718592 | tf_op jit(solution)/shard_map/reduce_scatter | solution.py:172
  36.0 19.9 %copy-start.14 = (f32[32]{0:T(128)}, f32[32]{0:T(128)S(1)}, u32[]{:S(2)}) copy-start(f32[32]{0:T(128)S(1)} %iota_convert_fusion) | copy-start | bytes 388
  53.0 6.2 %collective-permute-start = (bf16[256,512]{1,0:T(8,128)(2,1)S(1)}, bf16[256,512]{1,0:T(8,128)(2,1)S(1)}, u32[]{:S(2)}, u32[]{:S(2)}) collective-permute-start(bf16[256,512]{1,0:T(8,128)(2,1)S(1)} %reshape.341), channel_id=1, source_target_pairs={{0,1},{1,2},{2,3},{3,4},{4,5},{5,6},{6,7},{7,0},{8,9},{9,10},{10,1... | collective-permute-start | bytes 786440 | tf_op jit(solution)/shard_map/ppermute | solution.py:22
  56.0 7.4 %collective-permute-start.1 = (bf16[256,512]{1,0:T(8,128)(2,1)S(1)}, bf16[256,512]{1,0:T(8,128)(2,1)S(1)}, u32[]{:S(2)}, u32[]{:S(2)}) collective-permute-start(bf16[256,512]{1,0:T(8,128)(2,1)S(1)} %reshape.341), channel_id=1, source_target_pairs={{0,7},{1,0},{2,1},{3,2},{4,3},{5,4},{6,5},{7,6},{8,15},{9,8},{10,9... | collective-permute-start | bytes 786440 | tf_op jit(solution)/shard_map/ppermute | solution.py:27
  59.2 7.0 %collective-permute-start.2 = (bf16[256,512]{1,0:T(8,128)(2,1)S(1)}, bf16[256,512]{1,0:T(8,128)(2,1)S(1)}, u32[]{:S(2)}, u32[]{:S(2)}) collective-permute-start(bf16[256,512]{1,0:T(8,128)(2,1)S(1)} %collective-permute-done), channel_id=1, source_target_pairs={{0,1},{1,2},{2,3},{3,4},{4,5},{5,6},{6,7},{7,0},{8,9},{9,10},{10,1... | collective-permute-start | bytes 786440 | tf_op jit(solution)/shard_map/ppermute | solution.py:22
  63.4 7.4 %collective-permute-start.3 = (bf16[256,512]{1,0:T(8,128)(2,1)S(1)}, bf16[256,512]{1,0:T(8,128)(2,1)S(1)}, u32[]{:S(2)}, u32[]{:S(2)}) collective-permute-start(bf16[256,512]{1,0:T(8,128)(2,1)S(1)} %collective-permute-done.1), channel_id=1, source_target_pairs={{0,7},{1,0},{2,1},{3,2},{4,3},{5,4},{6,5},{7,6},{8,15},{9,8},{10,9... | collective-permute-start | bytes 786440 | tf_op jit(solution)/shard_map/ppermute | solution.py:27
  66.2 7.0 %collective-permute-start.4 = (bf16[256,512]{1,0:T(8,128)(2,1)S(1)}, bf16[256,512]{1,0:T(8,128)(2,1)S(1)}, u32[]{:S(2)}, u32[]{:S(2)}) collective-permute-start(bf16[256,512]{1,0:T(8,128)(2,1)S(1)} %collective-permute-done.2), channel_id=1, source_target_pairs={{0,1},{1,2},{2,3},{3,4},{4,5},{5,6},{6,7},{7,0},{8,9},{9,10},{10,1... | collective-permute-start | bytes 786440 | tf_op jit(solution)/shard_map/ppermute | solution.py:22
  70.8 7.4 %collective-permute-start.5 = (bf16[256,512]{1,0:T(8,128)(2,1)S(1)}, bf16[256,512]{1,0:T(8,128)(2,1)S(1)}, u32[]{:S(2)}, u32[]{:S(2)}) collective-permute-start(bf16[256,512]{1,0:T(8,128)(2,1)S(1)} %collective-permute-done.3), channel_id=1, source_target_pairs={{0,7},{1,0},{2,1},{3,2},{4,3},{5,4},{6,5},{7,6},{8,15},{9,8},{10,9... | collective-permute-start | bytes 786440 | tf_op jit(solution)/shard_map/ppermute | solution.py:27
  73.2 7.0 %collective-permute-start.6 = (bf16[256,512]{1,0:T(8,128)(2,1)S(1)}, bf16[256,512]{1,0:T(8,128)(2,1)S(1)}, u32[]{:S(2)}, u32[]{:S(2)}) collective-permute-start(bf16[256,512]{1,0:T(8,128)(2,1)S(1)} %collective-permute-done.4), channel_id=1, source_target_pairs={{0,1},{1,2},{2,3},{3,4},{4,5},{5,6},{6,7},{7,0},{8,9},{9,10},{10,1... | collective-permute-start | bytes 786440 | tf_op jit(solution)/shard_map/ppermute | solution.py:22
  80.2 1.1 copy-start.8
  80.2 1.1 copy-start.9
  81.3 1.2 copy-start.2
  82.6 2.6 copy-start.1
  82.6 2.0 copy-start.3
  82.6 2.6 copy-start.4
  85.7 25.8 %copy-start.5 = (bf16[1024,256]{1,0:T(8,128)(2,1)S(1)}, bf16[1024,256]{1,0:T(8,128)(2,1)}, u32[]{:S(2)}) copy-start(bf16[1024,256]{1,0:T(8,128)(2,1)} %param.31) | copy-start | bytes 1572868
  86.2 26.4 %copy-start.6 = (bf16[1024,256]{1,0:T(8,128)(2,1)S(1)}, bf16[1024,256]{1,0:T(8,128)(2,1)}, u32[]{:S(2)}) copy-start(bf16[1024,256]{1,0:T(8,128)(2,1)} %param.33) | copy-start | bytes 1572868
  171.6 0.7 copy-start.7
  522.1 42.6 %copy-start.11 = (f32[512]{0:T(512)S(1)}, f32[512]{0:T(512)}, u32[]{:S(2)}) copy-start(f32[512]{0:T(512)} %param.39) | copy-start | bytes 6148
  522.1 43.9 %copy-start.15 = (f32[32]{0:T(128)S(1)}, f32[32]{0:T(128)}, u32[]{:S(2)}) copy-start(f32[32]{0:T(128)} %copy-done.14) | copy-start | bytes 388
  566.0 29.1 %copy-start.13 = (s32[32]{0:T(128)S(1)}, s32[32]{0:T(128)}, u32[]{:S(2)}) copy-start(s32[32]{0:T(128)} %copy-done.12) | copy-start | bytes 388
Sparse Core Ops, SparseCore 0:
  9.9 75.1 all-gather.8
  87.7 75.0 all-gather.10
  165.5 75.0 all-gather.6
  243.1 98.2 all-gather.14
  343.7 97.0 all-gather.16
  443.1 73.4 all-gather.12
  522.3 42.4 reduce-scatter.1
